TPU v7x, 128 devices: a whole 4x4x4 slice. The times are simulated.
128 devices in a mesh: segment: 8 (over x, core), blk: 16 (over y, z).
Axes of the slice: x: 4, y: 4, z: 4, core: 2. Of those that a mesh axis runs over, the one named last changes fastest.
Arguments:
- fresh: bfloat16 [256, 4096], replicated, may hold values from -6 to 6
- previous: bfloat16 [8, 256, 4096], P('segment'), may hold values from -6 to 6
- span_index: int32 [8], P('segment'), may hold values from 0 to 7
- cache_counts: int32 [8, 16], P('segment'), may hold values from 1 to 2048, 16384 in all within a row
- norm_gain: float32 [8, 4096], P('segment'), may hold values from 0.1 to 1.9
- w_query: bfloat16 [8, 4096, 4096], P('segment', None, 'blk'), may hold values from -0.375 to 0.375
- w_keyval: bfloat16 [8, 4096, 2048], P('segment', None, 'blk'), may hold values from -0.09375 to 0.09375
- w_out: bfloat16 [8, 4096, 4096], P('segment', 'blk'), may hold values from -0.09375 to 0.09375
- cache_keys: bfloat16 [8, 32768, 1024], P('segment', 'blk'), may hold values from -220 to 220
- cache_values: bfloat16 [8, 32768, 1024], P('segment', 'blk'), may hold values from -6 to 6
Outputs:
- mixed: bfloat16 [8, 256, 4096], P('segment')
Inputs may be any that keep to these rules, and one draw needn't show every extreme that they name: Each row of cache_counts sums to 16384 and its largest entry is 2048.
All inputs are finite; a program needn't handle non-finite values.
Results may differ from a plain program's by a relative error of at most 0.012.
Values may be sent and summed in bfloat16 or wider, within the bound.
No kernel may reach another device: no remote copies, remote signals or barrier semaphores. Data moves between devices by JAX's collectives and lax.ppermute only.
A program may use at most 128 MiB of HBM per device.

v0:
```python
import jax
import jax.numpy as jnp
from jax import lax
from jax.sharding import PartitionSpec as P

KVH = 8
HD = 128
ROPE_BASE = 500000.0
EPSILON = 1e-05


def passed_along(block, axis, distance):
    devices = range(lax.axis_size(axis))
    route = [(i - distance, i) for i in devices if i - distance in devices]
    return lax.ppermute(block, axis, route)


def swapped(block, axis, distance):
    count = lax.axis_size(axis)
    route = []
    for low in range(count):
        high = low | 1 << distance
        if high != low and high < count:
            route += [(low, high), (high, low)]
    return lax.ppermute(block, axis, route)


def rotate(projected, first_span):
    length = projected.shape[0]
    half_width = projected.shape[-1] // 2
    positions = (first_span * length + jnp.arange(length, dtype=jnp.int32)).astype(jnp.float32)
    inverse = ROPE_BASE ** (
        -(jnp.arange(half_width, dtype=jnp.float32) * 2.0) / projected.shape[-1]
    )
    angles = positions[:, None] * inverse[None, :]
    cosine = jnp.cos(angles)[:, None, :]
    sine_table = jnp.sin(angles)[:, None, :]
    left_part = projected[..., :half_width]
    right_part = projected[..., half_width:]
    return jnp.concatenate(
        [
            left_part * cosine - right_part * sine_table,
            right_part * cosine + left_part * sine_table,
        ],
        axis=-1,
    )


def attend_rows(query_rows, key_rows, value_rows, allowed):
    scores = lax.dot_general(
        query_rows, key_rows, (((1,), (1,)), ((), ())), preferred_element_type=jnp.float32
    ) * query_rows.shape[-1] ** (-0.5)
    scores = jnp.where(allowed, scores, -jnp.inf)
    highest = jnp.max(scores, axis=-1, keepdims=True)
    weights = jnp.exp(scores - highest)
    totals = jnp.sum(weights, axis=-1, keepdims=True)
    partial_out = (
        jnp.dot(weights.astype(jnp.bfloat16), value_rows, preferred_element_type=jnp.float32)
        / totals
    ).astype(jnp.bfloat16)
    return (partial_out, (highest + jnp.log(totals))[:, 0])


def shards(
    fresh,
    previous,
    span_index,
    cache_counts,
    norm_gain,
    w_query,
    w_keyval,
    w_out,
    cache_keys,
    cache_values,
):
    blocks = lax.axis_size("blk")
    position = lax.axis_index("blk")
    span_rows = fresh.shape[0]
    arrived = passed_along(previous[0], "segment", 1)
    current = jnp.where(lax.axis_index("segment") == 0, fresh, arrived)
    widened = current.astype(jnp.float32)
    normed = (
        widened
        * lax.rsqrt(jnp.mean(widened * widened, axis=-1, keepdims=True) + EPSILON)
        * norm_gain[0]
    ).astype(jnp.bfloat16)
    first_span = span_index[0]
    heads_here = w_query.shape[2] // HD
    ratio = blocks // KVH
    queries = jnp.dot(normed, w_query[0], preferred_element_type=jnp.float32).reshape(
        span_rows, heads_here, HD
    )
    queries = rotate(queries, first_span).astype(jnp.bfloat16).reshape(span_rows, heads_here * HD)
    projected = jnp.dot(normed, w_keyval[0], preferred_element_type=jnp.float32)
    odd_member = position % 2 == 1
    as_key = rotate(projected[:, None, :], first_span)[:, 0, :].astype(jnp.bfloat16)
    mine = jnp.where(odd_member, projected.astype(jnp.bfloat16), as_key)
    partner = swapped(mine, "blk", 0)
    own_keys = jnp.where(odd_member, partner, mine)
    own_values = jnp.where(odd_member, mine, partner)
    query_rows = queries.reshape(span_rows * heads_here, HD)
    row_tokens = jnp.arange(span_rows * heads_here, dtype=jnp.int32) // heads_here
    causal = row_tokens[:, None] >= jnp.arange(span_rows, dtype=jnp.int32)[None, :]
    own_out, own_log = attend_rows(query_rows, own_keys, own_values, causal)
    own_out = own_out.reshape(span_rows, heads_here * HD)
    own_log = own_log.reshape(span_rows, heads_here).T
    cache_rows = cache_keys.shape[1]
    offsets = jnp.arange(cache_rows, dtype=jnp.int32)
    every_query = lax.all_gather(queries, "blk", axis=0, tiled=True)
    live = cache_counts[0, position]

    def holder(source):
        query_block = lax.dynamic_slice_in_dim(
            every_query, source * span_rows, span_rows, 0
        ).reshape(span_rows * heads_here, HD)
        head_start = source // ratio * HD
        key_rows = lax.dynamic_slice_in_dim(cache_keys[0], head_start, HD, 1)
        value_rows = lax.dynamic_slice_in_dim(cache_values[0], head_start, HD, 1)
        partial_out, log_totals = attend_rows(
            query_block, key_rows, value_rows, (offsets < live)[None, :]
        )
        return (
            partial_out.reshape(span_rows, heads_here * HD),
            log_totals.reshape(span_rows, heads_here).T,
        )

    held_outs, held_logs = lax.map(holder, jnp.arange(blocks, dtype=jnp.int32))
    shard_outs = lax.all_to_all(held_outs, "blk", split_axis=0, concat_axis=0, tiled=True)
    shard_logs = lax.all_to_all(held_logs, "blk", split_axis=0, concat_axis=0, tiled=True)
    all_outs = (
        jnp.concatenate([own_out[None], shard_outs], axis=0)
        .astype(jnp.float32)
        .reshape(blocks + 1, span_rows, heads_here, HD)
    )
    all_logs = jnp.concatenate([own_log[None], shard_logs], axis=0).transpose(0, 2, 1)
    ceiling = jnp.max(all_logs, axis=0)
    factors = jnp.exp(all_logs - ceiling)
    attended = (
        jnp.sum(factors[..., None] * all_outs, axis=0) / jnp.sum(factors, axis=0)[..., None]
    ).astype(jnp.bfloat16)
    attended = attended.reshape(span_rows, heads_here * HD)
    head_terms = lax.optimization_barrier(
        jnp.dot(attended, w_out[0], preferred_element_type=jnp.float32).astype(jnp.bfloat16)
    ).astype(jnp.float32)
    summed = lax.psum(head_terms.astype(jnp.bfloat16), "blk").astype(jnp.float32)
    mixed = (widened + summed).astype(jnp.bfloat16)
    return mixed[None]


def solution(mesh):
    placed = (
        P(),
        P("segment", None, None),
        P("segment"),
        P("segment", None),
        P("segment", None),
        P("segment", None, "blk"),
        P("segment", None, "blk"),
        P("segment", "blk", None),
        P("segment", "blk", None),
        P("segment", "blk", None),
    )
    return jax.shard_map(
        shards, mesh=mesh, in_specs=placed, out_specs=P("segment", None, None), check_vma=False
    )
```

profile of v0, /device:TPU:0, one launch (start us, length us, event | category | flops | bytes accessed | tf_op | source)
XLA Modules:
  0.0 425.8 jit_solution(5192613194957220926)
XLA Ops:
  6.5 2.8 collective-permute-start
  9.3 4.1 copy.33
  14.4 2.7 fusion.23
  19.9 67.0 %all-gather.2.cloned.1.call-done = bf16[4096,256]{1,0:T(8,128)(2,1)} async-done(((bf16[256,256]{1,0:T(8,128)(2,1)}), bf16[4096,256]{1,0:T(8,128)(2,1)}) %all-gather.2.cloned.1.call-update) | async-done | bytes 2097168 | tf_op jit(solution)/shard_map/all_gather | solution.py:109
  87.0 177.8 %while.15 = (s32[]{:T(128)}, bf16[16,256,256]{2,1,0:T(8,128)(2,1)}, f32[16,2,256]{2,1,0:T(2,128)S(1)}, s32[]{:T(128)}, s32[16]{0:T(128)S(1)}, /*index=5*/bf16[40...) while((s32[]{:T(128)}, bf16[16,256,256]{2,1,0:T(8,128)(2,1)}, ...), condition=%wide.region_6.7_spmd.clone, body=%wide.region_3.6_spmd.clone.sunk | while | flops 548537856 | bytes 14979499 | solution.py:127
  106.2 2.0 fusion.79
  117.3 2.0 fusion.79
  139.5 2.0 fusion.79
  150.6 2.0 fusion.79
  172.9 2.0 fusion.79
  206.2 2.0 fusion.79
  217.3 2.0 fusion.79
  239.6 2.0 fusion.79
  250.7 2.0 fusion.79
  264.8 12.4 %all_to_all.10 = f32[16,2,256]{2,1,0:T(2,128)S(1)} all-to-all(f32[16,2,256]{2,1,0:T(2,128)S(1)} %get-tuple-element.120), channel_id=1, replica_groups=mesh['segment'=8,'blk'=16] {'blk'}, dimensions={0} | all-to-all | bytes 65536 | tf_op jit(solution)/shard_map/all_to_all | solution.py:129
  277.2 4.4 %all-to-all-start.1 = ((bf16[16,256,256]{2,1,0:T(8,128)(2,1)}), bf16[16,256,256]{2,1,0:T(8,128)(2,1)}, u32[]{:S(2)}, u32[]{:S(2)}) async-start(bf16[16,256,256]{2,1,0:T(8,128)(2,1)} %get-tuple-element.121), calls=%async_computation.1 | async-start | bytes 4194304 | tf_op jit(solution)/shard_map/all_to_all | solution.py:128
  281.6 2.8 fusion.33
  286.9 18.0 %collective-permute-done.1 = bf16[256,128]{0,1:T(8,128)(2,1)S(1)} collective-permute-done((bf16[256,128]{0,1:T(8,128)(2,1)S(1)}, bf16[256,128]{0,1:T(8,128)(2,1)S(1)}, u32[]{:S(2)}, u32[]{:S(2)}) %collective-permute-start.1) | collective-permute-done | bytes 65568 | tf_op jit(solution)/shard_map/ppermute | solution.py:25
  306.0 2.1 copy.31
  309.4 4.0 concatenate.34
  313.4 7.7 %multiply_reduce_fusion = f32[256,2,128]{2,1,0:T(2,128)S(1)} fusion(bf16[16,256,2,128]{3,2,1,0:T(2,128)(2,1)} %concatenate.34, bf16[1,256,2,128]{3,2,1,0:T(2,128)(2,1)S(1)} %bitcast.73, f32[17,256,2]{2,1,0:T(8,128)} %copy.31), kind=kLoop, calls=%fused_computation.28 | loop fusion | flops 4390912 | bytes 2525184 | tf_op jit(solution)/shard_map/reduce_sum | solution.py:139
  321.5 2.0 convolution_convert_fusion
  323.5 91.1 %all-reduce.2.cloned.1.call-done = bf16[256,4096]{1,0:T(8,128)(2,1)} async-done(((bf16[256,4096]{1,0:T(8,128)(2,1)}), bf16[256,4096]{1,0:T(8,128)(2,1)}) %all-reduce.2.cloned.1.call-update) | async-done | bytes 2097168 | tf_op jit(solution)/shard_map/psum | solution.py:145
  414.6 4.3 %fusion.27 = bf16[1,256,4096]{2,1,0:T(8,128)(2,1)} fusion(bf16[256,4096]{1,0:T(8,128)(2,1)} %all-reduce.2.cloned.1.call-done, bf16[256,4096]{1,0:T(8,128)(2,1)} %copy-done.1), kind=kLoop, calls=%fused_computation.33 | loop fusion | flops 4194304 | bytes 6291456 | tf_op jit(solution)/shard_map/broadcast_in_dim | solution.py:147
  (243 shorter events, 117.4 us)
Async XLA Ops:
  6.5 314.9 %copy-start = (bf16[1,256,4096]{2,1,0:T(8,128)(2,1)S(1)}, bf16[1,256,4096]{2,1,0:T(8,128)(2,1)}, u32[]{:S(2)}) copy-start(bf16[1,256,4096]{2,1,0:T(8,128)(2,1)} %param.19) | copy-start | bytes 6291460
  6.5 80.4 %all-gather.2.cloned.1.call-start = ((), (), s32[]{:S(2)}) async-start(), calls=%async_computation.2 | async-start | bytes 2228224 | tf_op jit(solution)/shard_map/all_gather | solution.py:109
  6.5 7.9 %collective-permute-start = (bf16[256,4096]{1,0:T(8,128)(2,1)}, bf16[256,4096]{1,0:T(8,128)(2,1)}, u32[]{:S(2)}, u32[]{:S(2)}) collective-permute-start(bf16[256,4096]{1,0:T(8,128)(2,1)} %bitcast.76), channel_id=1, source_target_pairs={{0,16},{16,32},{32,48},{48,64},{64,80},{80,96},{96,112},{1,17},{17... | collective-permute-start | bytes 6291464 | tf_op jit(solution)/shard_map/ppermute | solution.py:15
  14.4 2.8 copy-start.2
  14.4 2.8 copy-start.3
  17.1 1.3 copy-start.1
  17.2 2.1 copy-start.4
  277.2 32.3 %all-to-all-start.1 = ((bf16[16,256,256]{2,1,0:T(8,128)(2,1)}), bf16[16,256,256]{2,1,0:T(8,128)(2,1)}, u32[]{:S(2)}, u32[]{:S(2)}) async-start(bf16[16,256,256]{2,1,0:T(8,128)(2,1)} %get-tuple-element.121), calls=%async_computation.1 | async-start | bytes 4194304 | tf_op jit(solution)/shard_map/all_to_all | solution.py:128
  281.6 133.0 %all-reduce.2.cloned.1.call-start = ((), (), s32[]{:S(2)}) async-start(), calls=%async_computation.3 | async-start | bytes 4194304 | tf_op jit(solution)/shard_map/psum | solution.py:145
  284.8 20.1 %collective-permute-start.1 = (bf16[256,128]{0,1:T(8,128)(2,1)S(1)}, bf16[256,128]{0,1:T(8,128)(2,1)S(1)}, u32[]{:S(2)}, u32[]{:S(2)}) collective-permute-start(bf16[256,128]{0,1:T(8,128)(2,1)S(1)} %fusion.54), channel_id=1, source_target_pairs={{0,1},{1,0},{2,3},{3,2},{4,5},{5,4},{6,7},{7,6},{8,9},{9,8},{10,11... | collective-permute-start | bytes 196616 | tf_op jit(solution)/shard_map/ppermute | solution.py:25
Sparse Core Ops, SparseCore 0:
  19.4 67.5 all-gather.1
  323.6 90.9 all-reduce.1
where the time goes:
time: 429 us; the launch traced here: 426 us
  waiting for transfers between devices  177 us (41%)
  matrix products  68.5 us (16%)
  local copies, waits for them, and re-layouts  52.7 us (12%)
  loops' own time  50.4 us (12%)
  other arithmetic  41.1 us (10%)
  between operations  14.3 us (3%)
  blocking collectives  12.4 us (3%)
  starting transfers between devices  9.06 us (2%)
    psum x1, waiting for transfers between devices, shards(): lax.psum(head_terms.astype(jnp.bfloat16), 'blk').astype(jnp.float32)  91.1 us
    all_gather x1, waiting for transfers between devices, shards(): every_query = lax.all_gather(queries, 'blk', axis=0, tiled=True)  67 us
    another operation x1, loops' own time, shards(): held_outs, held_logs = lax.map(holder, jnp.arange(blocks, dtype=jnp.int32))  50.4 us
    dot_general x17, matrix products, attend_rows(): jnp.dot(weights.astype(jnp.bfloat16), value_rows, preferred_element_type=...  32.6 us
    dot_general x17, matrix products, attend_rows(): lax.dot_general(query_rows, key_rows, (((1,), (1,)), ((), ())), preferred...  30.1 us
    ppermute x1, waiting for transfers between devices, swapped(): return lax.ppermute(block, axis, route)  18 us
    reduce_sum x17, other arithmetic, attend_rows(): totals = jnp.sum(weights, axis=-1, keepdims=True)  15.2 us
    dynamic_slice x16, local copies, waits for them, and re-layouts, holder(): lax.dynamic_slice_in_dim(every_query, source * span_rows, span_rows, 0)  14.7 us
  transfers between devices with their start and end apart: 5, of which 4 were waited for; matrix products, arithmetic and copies ran while one was open for 3% of the time, Pallas kernels for 0%

commit v1 on v0

--- a/solution.py
+++ b/solution.py
@@ -142,7 +142,12 @@
     head_terms = lax.optimization_barrier(
         jnp.dot(attended, w_out[0], preferred_element_type=jnp.float32).astype(jnp.bfloat16)
     ).astype(jnp.float32)
-    summed = lax.psum(head_terms.astype(jnp.bfloat16), "blk").astype(jnp.float32)
+
+    def series_compute(mine_x, axis_name):
+        near = jax.lax.all_gather(mine_x, axis_name).sum(axis=0)
+        return near
+
+    summed = series_compute(head_terms.astype(jnp.bfloat16), "blk").astype(jnp.float32)
     mixed = (widened + summed).astype(jnp.bfloat16)
     return mixed[None]
 

time: 429 us -> 550 us (1.28)
  waiting for transfers between devices: 177 us -> 284 us
  other arithmetic: 41.1 us -> 55.1 us
    all_gather x0 -> x1, waiting for transfers between devices: none -> 198 us  [series_compute(): near = jax.lax.all_gather(mine_x, axis_name).sum(axis=0)]
    psum x1 -> x0, waiting for transfers between devices: 91.1 us -> none  [shards(): lax.psum(head_terms.astype(jnp.bfloat16), 'blk').astype(jnp.float32)]
    reduce_sum x0 -> x1, other arithmetic: none -> 13 us  [series_compute(): near = jax.lax.all_gather(mine_x, axis_name).sum(axis=0)]
  transfers between devices with their start and end apart: 5 -> 5, of which waited for: 4 -> 4; matrix products, arithmetic and copies ran while one was open for 3% -> 2% of each run, Pallas kernels for 0% -> 0%
where the time goes in v1:
time: 550 us; the launch traced here: 547 us
  waiting for transfers between devices  284 us (52%)
  matrix products  68.4 us (12%)
  other arithmetic  55.1 us (10%)
  local copies, waits for them, and re-layouts  52.6 us (10%)
  loops' own time  50.5 us (9%)
  between operations  14.3 us (3%)
  blocking collectives  12.4 us (2%)
  starting transfers between devices  9.25 us (2%)
    all_gather x1, waiting for transfers between devices, series_compute(): near = jax.lax.all_gather(mine_x, axis_name).sum(axis=0)  198 us
    all_gather x1, waiting for transfers between devices, shards(): every_query = lax.all_gather(queries, 'blk', axis=0, tiled=True)  67 us
    another operation x1, loops' own time, shards(): held_outs, held_logs = lax.map(holder, jnp.arange(blocks, dtype=jnp.int32))  50.5 us
    dot_general x17, matrix products, attend_rows(): jnp.dot(weights.astype(jnp.bfloat16), value_rows, preferred_element_type=...  32.5 us
    dot_general x17, matrix products, attend_rows(): lax.dot_general(query_rows, key_rows, (((1,), (1,)), ((), ())), preferred...  30.1 us
    ppermute x1, waiting for transfers between devices, swapped(): return lax.ppermute(block, axis, route)  17.8 us
    reduce_sum x17, other arithmetic, attend_rows(): totals = jnp.sum(weights, axis=-1, keepdims=True)  15.2 us
    dynamic_slice x16, local copies, waits for them, and re-layouts, holder(): lax.dynamic_slice_in_dim(every_query, source * span_rows, span_rows, 0)  14.7 us
  transfers between devices with their start and end apart: 5, of which 4 were waited for; matrix products, arithmetic and copies ran while one was open for 2% of the time, Pallas kernels for 0%

profile of v1, /device:TPU:0, one launch (start us, length us, event | category | flops | bytes accessed | tf_op | source)
XLA Modules:
  0.0 546.5 jit_solution(4007755344468016487)
XLA Ops:
  6.5 2.8 collective-permute-start
  10.0 4.1 copy.33
  14.4 2.7 fusion.23
  20.0 67.0 %all-gather.4.cloned.1.call-done = bf16[4096,256]{1,0:T(8,128)(2,1)} async-done(((bf16[256,256]{1,0:T(8,128)(2,1)}), bf16[4096,256]{1,0:T(8,128)(2,1)}) %all-gather.4.cloned.1.call-update) | async-done | bytes 2097168 | tf_op jit(solution)/shard_map/all_gather | solution.py:109
  87.0 178.8 %while.15 = (s32[]{:T(128)}, bf16[16,256,256]{2,1,0:T(8,128)(2,1)}, f32[16,2,256]{2,1,0:T(2,128)S(1)}, s32[]{:T(128)}, s32[16]{0:T(128)S(1)}, /*index=5*/bf16[40...) while((s32[]{:T(128)}, bf16[16,256,256]{2,1,0:T(8,128)(2,1)}, ...), condition=%wide.region_6.7_spmd.clone, body=%wide.region_3.6_spmd.clone.sunk | while | flops 548537856 | bytes 14979499 | solution.py:127
  95.1 2.0 fusion.79
  106.3 2.0 fusion.79
  117.5 2.0 fusion.79
  139.8 2.0 fusion.79
  151.0 2.0 fusion.79
  162.2 2.0 fusion.79
  173.4 2.0 fusion.79
  184.5 2.0 fusion.79
  265.8 12.4 %all_to_all.10 = f32[16,2,256]{2,1,0:T(2,128)S(1)} all-to-all(f32[16,2,256]{2,1,0:T(2,128)S(1)} %get-tuple-element.120), channel_id=1, replica_groups=mesh['segment'=8,'blk'=16] {'blk'}, dimensions={0} | all-to-all | bytes 65536 | tf_op jit(solution)/shard_map/all_to_all | solution.py:129
  278.1 4.4 all-to-all-start.1
  282.6 2.8 fusion.33
  288.1 17.8 %collective-permute-done.1 = bf16[256,128]{0,1:T(8,128)(2,1)S(1)} collective-permute-done((bf16[256,128]{0,1:T(8,128)(2,1)S(1)}, bf16[256,128]{0,1:T(8,128)(2,1)S(1)}, u32[]{:S(2)}, u32[]{:S(2)}) %collective-permute-start.1) | collective-permute-done | bytes 65568 | tf_op jit(solution)/shard_map/ppermute | solution.py:25
  307.1 2.1 copy.31
  310.4 4.0 concatenate.34
  314.3 7.7 %multiply_reduce_fusion = f32[256,2,128]{2,1,0:T(2,128)S(1)} fusion(bf16[16,256,2,128]{3,2,1,0:T(2,128)(2,1)} %concatenate.34, bf16[1,256,2,128]{3,2,1,0:T(2,128)(2,1)S(1)} %bitcast.75, f32[17,256,2]{2,1,0:T(8,128)} %copy.31), kind=kLoop, calls=%fused_computation.28 | loop fusion | flops 4390912 | bytes 2525184 | tf_op jit(solution)/shard_map/reduce_sum | solution.py:139
  322.4 2.0 convolution_convert_fusion
  324.5 197.9 %all-gather.6.cloned.1.call-done = bf16[4096,4096]{1,0:T(8,128)(2,1)} async-done(((bf16[256,4096]{1,0:T(8,128)(2,1)}), bf16[4096,4096]{1,0:T(8,128)(2,1)}) %all-gather.6.cloned.1.call-update) | async-done | bytes 33554448 | tf_op jit(solution)/shard_map/all_gather | solution.py:147
  522.4 13.0 %reduce_sum.64 = bf16[256,4096]{1,0:T(8,128)(2,1)} reduce(bf16[16,256,4096]{2,1,0:T(8,128)(2,1)} %bitcast.67, bf16[]{:T(256)} %constant.139.clone.1), dimensions={0}, to_apply=%region_10.11 | reduce | flops 15728640 | bytes 35651584 | tf_op jit(solution)/shard_map/reduce_sum | solution.py:147
  535.4 4.3 fusion.27
  (244 shorter events, 120.6 us)
Async XLA Ops:
  6.5 315.9 %copy-start = (bf16[1,256,4096]{2,1,0:T(8,128)(2,1)S(1)}, bf16[1,256,4096]{2,1,0:T(8,128)(2,1)}, u32[]{:S(2)}) copy-start(bf16[1,256,4096]{2,1,0:T(8,128)(2,1)} %param.19) | copy-start | bytes 6291460
  6.5 80.4 %all-gather.4.cloned.1.call-start = ((), (), s32[]{:S(2)}) async-start(), calls=%async_computation.2 | async-start | bytes 2228224 | tf_op jit(solution)/shard_map/all_gather | solution.py:109
  6.5 7.9 %collective-permute-start = (bf16[256,4096]{1,0:T(8,128)(2,1)}, bf16[256,4096]{1,0:T(8,128)(2,1)}, u32[]{:S(2)}, u32[]{:S(2)}) collective-permute-start(bf16[256,4096]{1,0:T(8,128)(2,1)} %bitcast.78), channel_id=1, source_target_pairs={{0,16},{16,32},{32,48},{48,64},{64,80},{80,96},{96,112},{1,17},{17... | collective-permute-start | bytes 6291464 | tf_op jit(solution)/shard_map/ppermute | solution.py:15
  14.4 2.8 copy-start.2
  14.4 2.8 copy-start.3
  17.1 1.3 copy-start.1
  17.2 2.1 copy-start.4
  278.1 32.3 %all-to-all-start.1 = ((bf16[16,256,256]{2,1,0:T(8,128)(2,1)}), bf16[16,256,256]{2,1,0:T(8,128)(2,1)}, u32[]{:S(2)}, u32[]{:S(2)}) async-start(bf16[16,256,256]{2,1,0:T(8,128)(2,1)} %get-tuple-element.121), calls=%async_computation.1 | async-start | bytes 4194304 | tf_op jit(solution)/shard_map/all_to_all | solution.py:128
  282.6 239.8 %all-gather.6.cloned.1.call-start = ((), (), s32[]{:S(2)}) async-start(), calls=%async_computation.3 | async-start | bytes 35651584 | tf_op jit(solution)/shard_map/all_gather | solution.py:147
  285.8 20.1 %collective-permute-start.1 = (bf16[256,128]{0,1:T(8,128)(2,1)S(1)}, bf16[256,128]{0,1:T(8,128)(2,1)S(1)}, u32[]{:S(2)}, u32[]{:S(2)}) collective-permute-start(bf16[256,128]{0,1:T(8,128)(2,1)S(1)} %fusion.54), channel_id=1, source_target_pairs={{0,1},{1,0},{2,3},{3,2},{4,5},{5,4},{6,7},{7,6},{8,9},{9,8},{10,11... | collective-permute-start | bytes 196616 | tf_op jit(solution)/shard_map/ppermute | solution.py:25
Sparse Core Ops, SparseCore 0:
  19.4 67.5 all-gather.3
  324.6 197.7 all-gather.5
